TPU v7x, 256 devices: a whole 4x4x8 slice. The times are simulated.
256 devices in a mesh: tm: 2 (over core), tile: 128 (over x, z, y).
Axes of the slice: x: 4, y: 4, z: 8, core: 2. Of those that a mesh axis runs over, the one named last changes fastest.
Arguments:
- features: bfloat16 [4, 128, 128, 384], P('tm', 'tile'), may hold values from -48 to 48
- query_weight: bfloat16 [384, 384], replicated, may hold values from -1 to 1
- key_weight: bfloat16 [384, 384], replicated, may hold values from -12 to 12
- value_weight: bfloat16 [384, 384], replicated, may hold values from -0.3125 to 0.3125
- out_weight: bfloat16 [384, 384], replicated, may hold values from -1.25 to 1.25
- conv_weight: bfloat16 [3, 3, 3, 384, 384], replicated, may hold values from -0.0625 to 0.0625
Outputs:
- decoded: bfloat16 [4, 128, 128, 384], P('tm', 'tile')
All inputs are finite; a program needn't handle non-finite values.
Results may differ from a plain program's by a relative error of at most 0.019.
Values may be sent and summed in bfloat16 or wider, within the bound.
No kernel may reach another device: no remote copies, remote signals or barrier semaphores. Data moves between devices by JAX's collectives and lax.ppermute only.
A program may use at most 128 MiB of HBM per device.

v0:
```python
import math
import jax
import jax.numpy as jnp
from jax import lax
from jax.sharding import Mesh
from jax.sharding import PartitionSpec as P

ROW_AXES = ("x", "z", "y")


def rms_rows(values):
    return values * lax.rsqrt(jnp.mean(values * values, axis=-1, keepdims=True) + 1e-06)


def project(flat_rows, weight):
    return jnp.dot(flat_rows, weight, preferred_element_type=jnp.float32).astype(jnp.bfloat16)


def row_shift(block, forward):
    count = 1
    for name in ROW_AXES:
        count *= lax.axis_size(name)
    if forward:
        route = [(i, i + 1) for i in range(count - 1)]
    else:
        route = [(i + 1, i) for i in range(count - 1)]
    return lax.ppermute(block, ROW_AXES, route)


def per_device(features, query_weight, key_weight, value_weight, out_weight, conv_weight):
    frames, rows, cols, width = features.shape
    count = rows * cols
    widened = features.astype(jnp.float32)
    normed = rms_rows(widened).astype(jnp.bfloat16)
    flat = normed.reshape(frames * count, width)
    scale = 1.0 / math.sqrt(width)
    query = project(flat, query_weight).reshape(frames, count, width)
    query_all = lax.all_gather(query, "z", axis=1, tiled=True)
    normed_all = lax.all_gather(
        normed.reshape(frames, count, width), ("x", "y"), axis=1, tiled=True
    )
    keys_in = normed_all.reshape(-1, width)
    key_rows = project(keys_in, key_weight).reshape(frames, -1, width)
    value_rows = project(keys_in, value_weight).reshape(frames, -1, width)
    scores = (
        jnp.einsum("fqd,fkd->fqk", query_all, key_rows, preferred_element_type=jnp.float32) * scale
    )
    highest = lax.pmax(jnp.max(scores, axis=-1), "z")
    expo = jnp.exp(scores - highest[..., None])
    total = jnp.sum(expo, axis=-1)
    probs = expo.astype(jnp.bfloat16)
    summed = jnp.einsum("fqk,fkd->fqd", probs, value_rows, preferred_element_type=jnp.float32)
    summed = lax.psum_scatter(summed.astype(jnp.bfloat16), "z", scatter_dimension=1, tiled=True)
    total = lax.psum_scatter(total, "z", scatter_dimension=1, tiled=True)
    attended = (summed.astype(jnp.float32) / total[:, :, None]).astype(jnp.bfloat16)
    projected = jnp.dot(attended.reshape(-1, width), out_weight, preferred_element_type=jnp.float32)
    mixed = (widened + projected.reshape(features.shape)).astype(jnp.bfloat16)
    mixed_wide = mixed.astype(jnp.float32)
    activated = jax.nn.silu(rms_rows(mixed_wide)).astype(jnp.bfloat16)
    earlier = lax.ppermute(activated, "tm", [(0, 1)])
    stacked = jnp.concatenate([earlier, activated], axis=0)
    above = row_shift(stacked, True)
    below = row_shift(stacked, False)
    padded = jnp.concatenate([above, stacked, below], axis=1)
    padded = jnp.pad(padded, ((0, 0), (0, 0), (1, 1), (0, 0)))
    patches = []
    for tap_time in range(3):
        for tap_row in range(3):
            for tap_col in range(3):
                patches.append(
                    padded[
                        tap_time : tap_time + frames,
                        tap_row : tap_row + rows,
                        tap_col : tap_col + cols,
                    ]
                )
    columns = jnp.concatenate(patches, axis=-1).reshape(frames * count, 27 * width)
    conv = jnp.dot(
        columns, conv_weight.reshape(27 * width, width), preferred_element_type=jnp.float32
    )
    return (mixed_wide + conv.reshape(features.shape)).astype(jnp.bfloat16)


def solution(mesh):
    sizes = dict(zip(mesh.axis_names, mesh.devices.shape))
    tile = sizes["tile"]
    y = 4
    z = 8
    x = tile // (y * z)
    fine = Mesh(mesh.devices.reshape(sizes["tm"], x, z, y), ("tm", *ROW_AXES))
    spec = P("tm", ROW_AXES, None, None)
    in_specs = (spec, P(), P(), P(), P(), P())
    return jax.shard_map(per_device, mesh=fine, in_specs=in_specs, out_specs=spec, check_vma=False)
```

profile of v0, /device:TPU:6, one launch (start us, length us, event | category | flops | bytes accessed | tf_op | source)
XLA Modules:
  0.0 259.3 jit_solution(6664018388497770649)
XLA Ops:
  6.5 1.1 fusion.30
  7.6 1.7 fusion.31
  9.4 2.0 convolution_convert_fusion.2
  11.5 53.0 %all-gather.6.cloned.1.call-done = bf16[2,1,2048,384]{3,2,0,1:T(8,128)(2,1)} async-done(((bf16[2,1,128,384]{3,2,0,1:T(8,128)(2,1)}), bf16[2,1,2048,384]{3,2,0,1:T(8,128)(2,1)}) %all-gather.6.cloned.1.call-update) | async-done | bytes 3145744 | tf_op jit(solution)/shard_map/all_gather | solution.py:39
  64.5 5.7 %convolution_convert_fusion = bf16[4096,384]{1,0:T(8,128)(2,1)} fusion(bf16[4096,384]{1,0:T(8,128)(2,1)} %bitcast.58, bf16[384,384]{1,0:T(8,128)(2,1)S(1)} %copy-done), kind=kOutput, calls=%fused_computation.7 | convolution fusion | flops 1209532416 | bytes 6586368 | tf_op jit(solution)/shard_map/dot_general | solution.py:16
  70.3 2.1 convolution_convert_fusion.1
  72.4 33.3 %all-gather.4.cloned.1.call-done = bf16[2,1024,384]{2,1,0:T(8,128)(2,1)} async-done(((bf16[2,128,384]{2,1,0:T(8,128)(2,1)}), bf16[2,1024,384]{2,1,0:T(8,128)(2,1)}) %all-gather.4.cloned.1.call-update) | async-done | bytes 1572880 | tf_op jit(solution)/shard_map/all_gather | solution.py:38
  105.7 9.6 %multiply_reduce_fusion = (f32[2,1024]{1,0:T(2,128)S(1)}, f32[2,1024,2048]{2,1,0:T(8,128)}) fusion(bf16[2,1024,384]{2,1,0:T(8,128)(2,1)} %all-gather.4.cloned.1.call-done, bf16[2,2048,384]{2,1,0:T(8,128)(2,1)S(1)} %bitcast.60), kind=kOutput, calls=%fused_computation.1 | convolution fusion | flops 3229612032 | bytes 21504000 | tf_op jit(solution)/shard_map/fqd,fkd->fqk/dot_general | solution.py:46
  115.3 16.1 %pmax.7 = f32[2,1024]{1,0:T(2,128)S(1)} all-reduce(f32[2,1024]{1,0:T(2,128)S(1)} %get-tuple-element.5), channel_id=1, replica_groups=mesh['tm'=2,'x'=4,'z'=8,'y'=4] {'z'}, use_global_device_ids=true, to_apply=%region_2.0 | all-reduce | flops 2048 | bytes 16384 | tf_op jit(solution)/shard_map/pmax | solution.py:48
  131.4 7.7 %fusion = f32[2,1024]{1,0:T(2,128)S(1)} fusion(f32[2,1024,2048]{2,1,0:T(8,128)} %get-tuple-element.6, f32[2,1024]{1,0:T(2,128)S(1)} %pmax.7), kind=kLoop, calls=%fused_computation.2 | loop fusion | flops 12580864 | bytes 16793600 | tf_op jit(solution)/shard_map/reduce_sum | solution.py:50
  139.1 1.0 copy.11
  140.2 0.2 reduce-scatter.5.cloned.1.call-start
  140.4 11.5 %fusion.9 = bf16[2,1024,384]{2,1,0:T(8,128)(2,1)} fusion(bf16[2,2048,384]{2,1,0:T(8,128)(2,1)S(1)} %bitcast.61, f32[2,1024,2048]{2,1,0:T(8,128)} %get-tuple-element.6, f32[2,1024]{1,0:T(2,128)S(1)} %pmax.7), kind=kOutput, calls=%fused_computation.14 | convolution fusion | flops 3234594816 | bytes 21504000 | tf_op jit(solution)/shard_map/fqk,fkd->fqd/dot_general | solution.py:52
  152.0 25.5 %reduce-scatter.7.cloned.1.call-done = f32[128,2]{1,0:T(8,128)} async-done(((f32[1024,2]{1,0:T(8,128)}), f32[128,2]{1,0:T(8,128)}) %reduce-scatter.7.cloned.1.call-update) | async-done | bytes 1040
  177.5 0.9 copy.12
  178.3 40.8 %reduce-scatter.5.cloned.1.call-done = bf16[2,128,384]{2,1,0:T(8,128)(2,1)} async-done(((bf16[2,1024,384]{2,1,0:T(8,128)(2,1)}), bf16[2,128,384]{2,1,0:T(8,128)(2,1)}) %reduce-scatter.5.cloned.1.call-update) | async-done | bytes 196624 | tf_op jit(solution)/shard_map/reduce_scatter | solution.py:53
  219.1 1.7 multiply_reduce_fusion.1
  220.8 0.2 multiply_convert_fusion
  221.0 1.3 collective-permute-start
  222.3 1.0 collective-permute-done
  223.4 5.8 %collective-permute-start.2 = (bf16[4,1,128,384]{3,2,0,1:T(8,128)(2,1)S(1)}, bf16[4,1,128,384]{3,2,0,1:T(8,128)(2,1)S(1)}, u32[]{:S(2)}, u32[]{:S(2)}) collective-permute-start(bf16[4,1,128,384]{3,2,0,1:T(8,128)(2,1)S(1)} %pad_maximum_fusion), channel_id=1, source_target_pairs={{1,0},{2,1},{3,2},{4,3},{5,4},{6,5},{7,6},{8,7},{9,8},{10,9},{11,1... | collective-permute-start | bytes 1179656 | tf_op jit(solution)/shard_map/ppermute | solution.py:27
  229.2 1.9 collective-permute-start.1
  231.2 7.0 %collective-permute-done.2 = bf16[4,1,128,384]{3,2,0,1:T(8,128)(2,1)S(1)} collective-permute-done((bf16[4,1,128,384]{3,2,0,1:T(8,128)(2,1)S(1)}, bf16[4,1,128,384]{3,2,0,1:T(8,128)(2,1)S(1)}, u32[]{:S(2)}, u32[]{:S(2)}) %collective-permute-start.2) | collective-permute-done | bytes 393248 | tf_op jit(solution)/shard_map/ppermute | solution.py:27
  238.1 8.3 %collective-permute-done.1 = bf16[4,1,128,384]{3,2,0,1:T(8,128)(2,1)S(1)} collective-permute-done((bf16[4,1,128,384]{3,2,0,1:T(8,128)(2,1)S(1)}, bf16[4,1,128,384]{3,2,0,1:T(8,128)(2,1)S(1)}, u32[]{:S(2)}, u32[]{:S(2)}) %collective-permute-start.1) | collective-permute-done | bytes 393248 | tf_op jit(solution)/shard_map/ppermute | solution.py:27
  246.5 0.3 select_maximum_fusion
  246.9 0.1 slice_dynamic-update-slice_fusion.21
  247.0 0.1 slice_dynamic-update-slice_fusion.19
  247.2 0.1 slice_dynamic-update-slice_fusion.16
  247.6 0.1 slice_dynamic-update-slice_fusion.8
  247.9 0.2 constant_dynamic-update-slice_fusion
  248.3 0.8 slice-done.1
  249.1 3.6 %fusion.27 = bf16[2,1,128,384]{3,2,1,0:T(8,128)(2,1)} fusion(f32[2,1,128,384]{3,2,0,1:T(8,128)S(1)} %get-tuple-element.8, bf16[10368,384,1]{1,0,2:T(8,128)(2,1)S(1)} %bitcast.68, bf16[2,1,128,10368]{3,2,0,1:T(8,128)(2,1)S(1)} %slice_dynamic-update-slice_fusion), kind=kOutput, calls=%fused_computation.28 | convolution fusion | flops 2038628352 | bytes 13860864 | tf_op jit(solution)/shard_map/dot_general | solution.py:78
  (44 shorter events, 1.1 us)
Async XLA Ops:
  6.5 58.0 %copy-start = (bf16[384,384]{1,0:T(8,128)(2,1)S(1)}, bf16[384,384]{1,0:T(8,128)(2,1)}, u32[]{:S(2)}) copy-start(bf16[384,384]{1,0:T(8,128)(2,1)} %param.9) | copy-start | bytes 884740
  6.5 58.0 %all-gather.6.cloned.1.call-start = ((), (), s32[]{:S(2)}) async-start(), calls=%async_computation.4 | async-start | bytes 3342336 | tf_op jit(solution)/shard_map/all_gather | solution.py:39
  9.4 96.3 %all-gather.4.cloned.1.call-start = ((), (), s32[]{:S(2)}) async-start(), calls=%async_computation.2 | async-start | bytes 1769472 | tf_op jit(solution)/shard_map/all_gather | solution.py:38
  11.5 166.0 %reduce-scatter.7.cloned.1.call-start = ((), (), s32[]{:S(2)}) async-start(), calls=%async_computation.5 | async-start | bytes 589824
  64.5 5.7 %copy-start.1 = (bf16[2,1,2048,384]{3,2,0,1:T(8,128)(2,1)S(1)}, bf16[2,1,2048,384]{3,2,0,1:T(8,128)(2,1)}, u32[]{:S(2)}) copy-start(bf16[2,1,2048,384]{3,2,0,1:T(8,128)(2,1)} %all-gather.6.cloned.1.call-done) | copy-start | bytes 9437188
  64.5 5.8 %copy-start.3 = (bf16[384,384]{1,0:T(8,128)(2,1)S(1)}, bf16[384,384]{1,0:T(8,128)(2,1)}, u32[]{:S(2)}) copy-start(bf16[384,384]{1,0:T(8,128)(2,1)} %param.8) | copy-start | bytes 884740
  131.4 9.0 %copy-start.2 = (bf16[4096,384]{1,0:T(8,128)(2,1)S(1)}, bf16[4096,384]{1,0:T(8,128)(2,1)}, u32[]{:S(2)}) copy-start(bf16[4096,384]{1,0:T(8,128)(2,1)} %convolution_convert_fusion) | copy-start | bytes 9437188
  140.2 79.0 %reduce-scatter.5.cloned.1.call-start = ((), (), s32[]{:S(2)}) async-start(), calls=%async_computation.3 | async-start | bytes 1769472 | tf_op jit(solution)/shard_map/reduce_scatter | solution.py:53
  219.1 29.2 %slice-start = ((s8[7962624]{0:T(1024)(128)(4,1)}), s8[4194304]{0:T(1024)(128)(4,1)S(1)}, s32[]{:S(2)}) async-start(s8[7962624]{0:T(1024)(128)(4,1)} %bitcast.66), calls=%async_computation.6 | async-start | bytes 8388608
  221.0 2.4 collective-permute-start
  223.4 14.7 %collective-permute-start.2 = (bf16[4,1,128,384]{3,2,0,1:T(8,128)(2,1)S(1)}, bf16[4,1,128,384]{3,2,0,1:T(8,128)(2,1)S(1)}, u32[]{:S(2)}, u32[]{:S(2)}) collective-permute-start(bf16[4,1,128,384]{3,2,0,1:T(8,128)(2,1)S(1)} %pad_maximum_fusion), channel_id=1, source_target_pairs={{1,0},{2,1},{3,2},{4,3},{5,4},{6,5},{7,6},{8,7},{9,8},{10,9},{11,1... | collective-permute-start | bytes 1179656 | tf_op jit(solution)/shard_map/ppermute | solution.py:27
  229.2 17.2 %collective-permute-start.1 = (bf16[4,1,128,384]{3,2,0,1:T(8,128)(2,1)S(1)}, bf16[4,1,128,384]{3,2,0,1:T(8,128)(2,1)S(1)}, u32[]{:S(2)}, u32[]{:S(2)}) collective-permute-start(bf16[4,1,128,384]{3,2,0,1:T(8,128)(2,1)S(1)} %pad_maximum_fusion), channel_id=1, source_target_pairs={{0,1},{1,2},{2,3},{3,4},{4,5},{5,6},{6,7},{7,8},{8,9},{9,10},{10,1... | collective-permute-start | bytes 1179656 | tf_op jit(solution)/shard_map/ppermute | solution.py:27
  247.1 2.1 slice-start.1
Sparse Core Ops, SparseCore 0:
  9.8 54.7 all-gather.5
  66.3 39.3 all-gather.3
  140.3 37.1 reduce-scatter.6
  179.9 39.2 reduce-scatter.4
where the time goes:
time: 260 us; the launch traced here: 259 us
  waiting for transfers between devices  169 us (65%)
  matrix products  36.3 us (14%)
  blocking collectives  16.1 us (6%)
  between operations  13.4 us (5%)
  other arithmetic  11.4 us (4%)
  starting transfers between devices  9.31 us (4%)
  local copies, waits for them, and re-layouts  3.88 us (1%)
    all_gather x1, waiting for transfers between devices, per_device(): lax.all_gather(normed.reshape(frames, count, width), ('x', 'y'), axis=1,...  53 us
    reduce_scatter x1, waiting for transfers between devices, per_device(): lax.psum_scatter(summed.astype(jnp.bfloat16), 'z', scatter_dimension=1, t...  40.8 us
    all_gather x1, waiting for transfers between devices, per_device(): query_all = lax.all_gather(query, 'z', axis=1, tiled=True)  33.3 us
    unnamed x5, waiting for transfers between devices  25.5 us
    pmax x1, blocking collectives, per_device(): highest = lax.pmax(jnp.max(scores, axis=-1), 'z')  16.1 us
    ppermute x2, waiting for transfers between devices, row_shift(): return lax.ppermute(block, ROW_AXES, route)  15.3 us
    dot_general x1, matrix products, per_device(): jnp.einsum('fqk,fkd->fqd', probs, value_rows, preferred_element_type=jnp....  11.5 us
    dot_general x3, matrix products, project(): jnp.dot(flat_rows, weight, preferred_element_type=jnp.float32)  9.84 us
  transfers between devices with their start and end apart: 7, of which 7 were waited for; matrix products, arithmetic and copies ran while one was open for 9% of the time, Pallas kernels for 0%

commit v1 on v0

--- a/solution.py
+++ b/solution.py
@@ -36,9 +36,13 @@
     scale = 1.0 / math.sqrt(width)
     query = project(flat, query_weight).reshape(frames, count, width)
     query_all = lax.all_gather(query, "z", axis=1, tiled=True)
-    normed_all = lax.all_gather(
-        normed.reshape(frames, count, width), ("x", "y"), axis=1, tiled=True
+    _find_screen = lambda u, mesh_ax: jnp.concatenate(
+        lax.all_to_all(
+            jnp.stack([u for _ in range(lax.axis_size(mesh_ax))], axis=0), mesh_ax, 0, 0
+        ),
+        1,
     )
+    normed_all = _find_screen(normed.reshape(frames, count, width), ("x", "y"))
     keys_in = normed_all.reshape(-1, width)
     key_rows = project(keys_in, key_weight).reshape(frames, -1, width)
     value_rows = project(keys_in, value_weight).reshape(frames, -1, width)

time: 260 us -> 224 us (0.86)
  waiting for transfers between devices: 169 us -> 121 us
  starting transfers between devices: 9.31 us -> 16.7 us
  blocking collectives: 16.1 us -> 20.2 us
    all_gather x1 -> x0, waiting for transfers between devices: 53 us -> none  [per_device(): lax.all_gather(normed.reshape(frames, count, width), ('x', 'y'), axis=1,...]
    all_to_all x0 -> x1, waiting for transfers between devices: none -> 38.7 us  [per_device(): lax.all_to_all(jnp.stack([u for _ in range(lax.axis_size(mesh_ax))], axis...]
    all_gather x1, waiting for transfers between devices: 33.3 us -> 0.02 us  [per_device(): query_all = lax.all_gather(query, 'z', axis=1, tiled=True)]
    all_to_all x0 -> x1, starting transfers between devices: none -> 7.43 us  [per_device(): lax.all_to_all(jnp.stack([u for _ in range(lax.axis_size(mesh_ax))], axis...]
    pmax x1, blocking collectives: 16.1 us -> 20.2 us  [per_device(): highest = lax.pmax(jnp.max(scores, axis=-1), 'z')]
    unnamed x5 -> x4, waiting for transfers between devices: 25.5 us -> 25.3 us
  transfers between devices with their start and end apart: 7 -> 7, of which waited for: 7 -> 6; matrix products, arithmetic and copies ran while one was open for 9% -> 10% of each run, Pallas kernels for 0% -> 0%
where the time goes in v1:
time: 224 us
  waiting for transfers between devices  121 us (54%)
  matrix products  34.1 us (15%)
  blocking collectives  20.2 us (9%)
  starting transfers between devices  16.7 us (7%)
  between operations  13.4 us (6%)
  other arithmetic  11.7 us (5%)
  local copies, waits for them, and re-layouts  6.36 us (3%)
    reduce_scatter x1, waiting for transfers between devices, per_device(): lax.psum_scatter(summed.astype(jnp.bfloat16), 'z', scatter_dimension=1, t...  40.8 us
    all_to_all x1, waiting for transfers between devices, per_device(): lax.all_to_all(jnp.stack([u for _ in range(lax.axis_size(mesh_ax))], axis...  38.7 us
    unnamed x4, waiting for transfers between devices  25.3 us
    pmax x1, blocking collectives, per_device(): highest = lax.pmax(jnp.max(scores, axis=-1), 'z')  20.2 us
    ppermute x2, waiting for transfers between devices, row_shift(): return lax.ppermute(block, ROW_AXES, route)  15.3 us
    dot_general x1, matrix products, per_device(): jnp.einsum('fqk,fkd->fqd', probs, value_rows, preferred_element_type=jnp....  11.5 us
    dot_general x1, matrix products, per_device(): jnp.einsum('fqd,fkd->fqk', query_all, key_rows, preferred_element_type=jn...  9.6 us
    reduce_sum x1, other arithmetic, per_device(): total = jnp.sum(expo, axis=-1)  7.74 us
  transfers between devices with their start and end apart: 7, of which 6 were waited for; matrix products, arithmetic and copies ran while one was open for 10% of the time, Pallas kernels for 0%

profile of v1, /device:TPU:6, one launch (start us, length us, event | category | flops | bytes accessed | tf_op | source)
XLA Modules:
  0.0 223.7 jit_solution(15122097797884886967)
XLA Ops:
  6.5 1.1 fusion.30
  7.6 1.0 fusion.47
  8.7 2.1 stack.3
  10.8 7.4 %all-to-all-start = ((bf16[16,2,128,384]{3,2,1,0:T(8,128)(2,1)}), bf16[16,2,128,384]{3,2,1,0:T(8,128)(2,1)S(1)}, u32[]{:S(2)}, u32[]{:S(2)}) async-start(bf16[16,2,128,384]{3,2,1,0:T(8,128)(2,1)} %stack.3), calls=%async_computation | async-start | bytes 6291456 | tf_op jit(solution)/shard_map/all_to_all | solution.py:40
  18.3 1.0 fusion.31
  19.3 1.9 convolution_convert_fusion.2
  21.3 38.7 %all-to-all-done = bf16[16,2,128,384]{3,2,1,0:T(8,128)(2,1)S(1)} async-done(((bf16[16,2,128,384]{3,2,1,0:T(8,128)(2,1)}), bf16[16,2,128,384]{3,2,1,0:T(8,128)(2,1)S(1)}, u32[]{:S(2)}, u32[]{:S(2)}) %all-to-all-start) | async-done | bytes 3145760 | tf_op jit(solution)/shard_map/all_to_all | solution.py:40
  60.0 0.3 copy.12
  60.4 3.7 %convolution_convert_fusion = bf16[4096,384]{1,0:T(8,128)(2,1)} fusion(bf16[4096,384]{1,0:T(8,128)(2,1)S(1)} %bitcast.64, bf16[384,384]{1,0:T(8,128)(2,1)S(1)} %copy-done), kind=kOutput, calls=%fused_computation.7 | convolution fusion | flops 1209532416 | bytes 6586368 | tf_op jit(solution)/shard_map/dot_general | solution.py:16
  64.1 2.1 convolution_convert_fusion.1
  66.2 9.6 %multiply_reduce_fusion = (f32[2,1024]{1,0:T(2,128)S(1)}, f32[2,1024,2048]{2,1,0:T(8,128)}) fusion(bf16[2,1024,384]{2,1,0:T(8,128)(2,1)} %all-gather.2.cloned.1.call-done, bf16[2,2048,384]{2,1,0:T(8,128)(2,1)S(1)} %bitcast.66), kind=kOutput, calls=%fused_computation.1 | convolution fusion | flops 3229612032 | bytes 21504000 | tf_op jit(solution)/shard_map/fqd,fkd->fqk/dot_general | solution.py:50
  75.8 20.2 %pmax.7 = f32[2,1024]{1,0:T(2,128)S(1)} all-reduce(f32[2,1024]{1,0:T(2,128)S(1)} %get-tuple-element.5), channel_id=1, replica_groups=mesh['tm'=2,'x'=4,'z'=8,'y'=4] {'z'}, use_global_device_ids=true, to_apply=%region_2.0 | all-reduce | flops 2048 | bytes 16384 | tf_op jit(solution)/shard_map/pmax | solution.py:52
  96.0 7.7 %fusion = f32[2,1024]{1,0:T(2,128)S(1)} fusion(f32[2,1024,2048]{2,1,0:T(8,128)} %get-tuple-element.6, f32[2,1024]{1,0:T(2,128)S(1)} %pmax.7), kind=kLoop, calls=%fused_computation.2 | loop fusion | flops 12580864 | bytes 16793600 | tf_op jit(solution)/shard_map/reduce_sum | solution.py:54
  103.8 1.0 copy.14
  104.8 0.2 reduce-scatter.5.cloned.1.call-start
  105.1 11.5 %fusion.9 = bf16[2,1024,384]{2,1,0:T(8,128)(2,1)} fusion(bf16[2,2048,384]{2,1,0:T(8,128)(2,1)S(1)} %bitcast.67, f32[2,1024,2048]{2,1,0:T(8,128)} %get-tuple-element.6, f32[2,1024]{1,0:T(2,128)S(1)} %pmax.7), kind=kOutput, calls=%fused_computation.14 | convolution fusion | flops 3234594816 | bytes 21504000 | tf_op jit(solution)/shard_map/fqk,fkd->fqd/dot_general | solution.py:56
  116.6 25.3 %reduce-scatter.7.cloned.1.call-done = f32[128,2]{1,0:T(8,128)} async-done(((f32[1024,2]{1,0:T(8,128)}), f32[128,2]{1,0:T(8,128)}) %reduce-scatter.7.cloned.1.call-update) | async-done | bytes 1040
  141.9 0.9 copy.15
  142.8 40.8 %reduce-scatter.5.cloned.1.call-done = bf16[2,128,384]{2,1,0:T(8,128)(2,1)} async-done(((bf16[2,1024,384]{2,1,0:T(8,128)(2,1)}), bf16[2,128,384]{2,1,0:T(8,128)(2,1)}) %reduce-scatter.5.cloned.1.call-update) | async-done | bytes 196624 | tf_op jit(solution)/shard_map/reduce_scatter | solution.py:57
  183.6 1.7 multiply_reduce_fusion.1
  185.3 0.2 multiply_convert_fusion
  185.5 1.3 collective-permute-start
  186.8 1.0 collective-permute-done
  187.9 5.7 %collective-permute-start.2 = (bf16[4,1,128,384]{3,2,0,1:T(8,128)(2,1)S(1)}, bf16[4,1,128,384]{3,2,0,1:T(8,128)(2,1)S(1)}, u32[]{:S(2)}, u32[]{:S(2)}) collective-permute-start(bf16[4,1,128,384]{3,2,0,1:T(8,128)(2,1)S(1)} %pad_maximum_fusion), channel_id=1, source_target_pairs={{1,0},{2,1},{3,2},{4,3},{5,4},{6,5},{7,6},{8,7},{9,8},{10,9},{11,1... | collective-permute-start | bytes 1179656 | tf_op jit(solution)/shard_map/ppermute | solution.py:27
  193.7 1.9 collective-permute-start.1
  195.6 7.0 %collective-permute-done.2 = bf16[4,1,128,384]{3,2,0,1:T(8,128)(2,1)S(1)} collective-permute-done((bf16[4,1,128,384]{3,2,0,1:T(8,128)(2,1)S(1)}, bf16[4,1,128,384]{3,2,0,1:T(8,128)(2,1)S(1)}, u32[]{:S(2)}, u32[]{:S(2)}) %collective-permute-start.2) | collective-permute-done | bytes 393248 | tf_op jit(solution)/shard_map/ppermute | solution.py:27
  202.6 8.3 %collective-permute-done.1 = bf16[4,1,128,384]{3,2,0,1:T(8,128)(2,1)S(1)} collective-permute-done((bf16[4,1,128,384]{3,2,0,1:T(8,128)(2,1)S(1)}, bf16[4,1,128,384]{3,2,0,1:T(8,128)(2,1)S(1)}, u32[]{:S(2)}, u32[]{:S(2)}) %collective-permute-start.1) | collective-permute-done | bytes 393248 | tf_op jit(solution)/shard_map/ppermute | solution.py:27
  210.9 0.3 select_maximum_fusion
  211.5 0.1 slice_dynamic-update-slice_fusion.19
  212.3 0.2 constant_dynamic-update-slice_fusion
  212.8 0.8 slice-done.1
  213.6 3.6 %fusion.27 = bf16[2,1,128,384]{3,2,1,0:T(8,128)(2,1)} fusion(f32[2,1,128,384]{3,2,0,1:T(8,128)S(1)} %get-tuple-element.8, bf16[10368,384,1]{1,0,2:T(8,128)(2,1)S(1)} %bitcast.74, bf16[2,1,128,10368]{3,2,0,1:T(8,128)(2,1)S(1)} %slice_dynamic-update-slice_fusion), kind=kOutput, calls=%fused_computation.28 | convolution fusion | flops 2038628352 | bytes 13860864 | tf_op jit(solution)/shard_map/dot_general | solution.py:82
  (44 shorter events, 1.3 us)
Async XLA Ops:
  6.5 53.8 %copy-start = (bf16[384,384]{1,0:T(8,128)(2,1)S(1)}, bf16[384,384]{1,0:T(8,128)(2,1)}, u32[]{:S(2)}) copy-start(bf16[384,384]{1,0:T(8,128)(2,1)} %param.9) | copy-start | bytes 884740
  10.8 49.2 %all-to-all-start = ((bf16[16,2,128,384]{3,2,1,0:T(8,128)(2,1)}), bf16[16,2,128,384]{3,2,1,0:T(8,128)(2,1)S(1)}, u32[]{:S(2)}, u32[]{:S(2)}) async-start(bf16[16,2,128,384]{3,2,1,0:T(8,128)(2,1)} %stack.3), calls=%async_computation | async-start | bytes 6291456 | tf_op jit(solution)/shard_map/all_to_all | solution.py:40
  18.2 48.0 %all-gather.2.cloned.1.call-start = ((), (), s32[]{:S(2)}) async-start(), calls=%async_computation.3 | async-start | bytes 1769472 | tf_op jit(solution)/shard_map/all_gather | solution.py:38
  21.2 120.6 %reduce-scatter.7.cloned.1.call-start = ((), (), s32[]{:S(2)}) async-start(), calls=%async_computation.5 | async-start | bytes 589824
  60.4 3.7 %copy-start.2 = (bf16[384,384]{1,0:T(8,128)(2,1)S(1)}, bf16[384,384]{1,0:T(8,128)(2,1)}, u32[]{:S(2)}) copy-start(bf16[384,384]{1,0:T(8,128)(2,1)} %param.8) | copy-start | bytes 884740
  96.0 9.0 %copy-start.1 = (bf16[4096,384]{1,0:T(8,128)(2,1)S(1)}, bf16[4096,384]{1,0:T(8,128)(2,1)}, u32[]{:S(2)}) copy-start(bf16[4096,384]{1,0:T(8,128)(2,1)} %convolution_convert_fusion) | copy-start | bytes 9437188
  104.8 78.8 %reduce-scatter.5.cloned.1.call-start = ((), (), s32[]{:S(2)}) async-start(), calls=%async_computation.4 | async-start | bytes 1769472 | tf_op jit(solution)/shard_map/reduce_scatter | solution.py:57
  183.6 29.1 %slice-start = ((s8[7962624]{0:T(1024)(128)(4,1)}), s8[4194304]{0:T(1024)(128)(4,1)S(1)}, s32[]{:S(2)}) async-start(s8[7962624]{0:T(1024)(128)(4,1)} %bitcast.72), calls=%async_computation.6 | async-start | bytes 8388608
  185.5 2.4 %collective-permute-start = (bf16[2,1,128,384]{3,2,0,1:T(8,128)(2,1)S(1)}, bf16[2,1,128,384]{3,2,0,1:T(8,128)(2,1)S(1)}, u32[]{:S(2)}, u32[]{:S(2)}) collective-permute-start(bf16[2,1,128,384]{3,2,0,1:T(8,128)(2,1)S(1)} %multiply_convert_fusion), channel_id=1, source_target_pairs={{0,128},{1,129},{2,130},{3,131},{4,132},{5,133},{6,134},{7,135},{8... | collective-permute-start | bytes 589832 | tf_op jit(solution)/shard_map/ppermute | solution.py:64
  187.9 14.6 %collective-permute-start.2 = (bf16[4,1,128,384]{3,2,0,1:T(8,128)(2,1)S(1)}, bf16[4,1,128,384]{3,2,0,1:T(8,128)(2,1)S(1)}, u32[]{:S(2)}, u32[]{:S(2)}) collective-permute-start(bf16[4,1,128,384]{3,2,0,1:T(8,128)(2,1)S(1)} %pad_maximum_fusion), channel_id=1, source_target_pairs={{1,0},{2,1},{3,2},{4,3},{5,4},{6,5},{7,6},{8,7},{9,8},{10,9},{11,1... | collective-permute-start | bytes 1179656 | tf_op jit(solution)/shard_map/ppermute | solution.py:27
  193.7 17.2 %collective-permute-start.1 = (bf16[4,1,128,384]{3,2,0,1:T(8,128)(2,1)S(1)}, bf16[4,1,128,384]{3,2,0,1:T(8,128)(2,1)S(1)}, u32[]{:S(2)}, u32[]{:S(2)}) collective-permute-start(bf16[4,1,128,384]{3,2,0,1:T(8,128)(2,1)S(1)} %pad_maximum_fusion), channel_id=1, source_target_pairs={{0,1},{1,2},{2,3},{3,4},{4,5},{5,6},{6,7},{7,8},{8,9},{9,10},{10,1... | collective-permute-start | bytes 1179656 | tf_op jit(solution)/shard_map/ppermute | solution.py:27
  211.5 2.1 slice-start.1
Sparse Core Ops, SparseCore 0:
  21.4 42.3 all-gather.1
  105.0 36.8 reduce-scatter.6
  144.4 39.1 reduce-scatter.4
